TPU v7x, 32 devices: a whole 2x2x4 slice. The times are simulated.
32 devices in a mesh: group: 2 (over y), inp: 4 (over z), tm: 2 (over x), pol: 2 (over core).
Axes of the slice: x: 2, y: 2, z: 4, core: 2. Of those that a mesh axis runs over, the one named last changes fastest.
Arguments:
- voltages: bfloat16 [1024, 65536], P(('group', 'inp'), ('tm', 'pol')), parts along dimension 0, may hold values from -6 to 6
Outputs:
- visibilities: float32 [1024, 2, 512, 512], P(('group', 'inp', 'tm'), None, 'pol'), parts along dimension 0
There are 2 independent parts, one for each index of `group`. A program takes and returns all parts, laid end to end along the dimension named above; each array names one. Nothing has to cross between parts.
All inputs are finite; a program needn't handle non-finite values.
Results may differ from a plain program's by a relative error of at most 0.0054.
Values may be sent and summed in bfloat16 or wider, within the bound.
No kernel may reach another device: no remote copies, remote signals or barrier semaphores. Data moves between devices by JAX's collectives and lax.ppermute only.
A program may use at most 256 MiB of HBM per device.

v0:
```python
import math
import jax
import jax.numpy as jnp
from jax import lax
from jax.sharding import PartitionSpec as P

CH = 512
TAPS = 16


def shifted(block, axis, distance):
    devices = range(lax.axis_size(axis))
    route = [(i - distance, i) for i in devices if i - distance in devices]
    return lax.ppermute(block, axis, route)


def prototype(tap_count, frame_len):
    length = tap_count * frame_len
    sample = lax.broadcasted_iota(jnp.int32, (length,), 0).astype(jnp.float32)
    centred = (sample - (length - 1) / 2.0) / frame_len
    window = 0.5 - 0.5 * jnp.cos(2.0 * math.pi * (sample + 0.5) / length)
    angle = math.pi * centred
    filter_taps = jnp.sin(angle) / angle * window
    filter_taps = filter_taps / jnp.sqrt(jnp.sum(filter_taps * filter_taps))
    return filter_taps.reshape(tap_count, frame_len)


def dft_table(frame_len):
    sample_idx = lax.broadcasted_iota(jnp.int32, (frame_len, frame_len // 2), 0)
    channel_idx = lax.broadcasted_iota(jnp.int32, (frame_len, frame_len // 2), 1)
    phase = (sample_idx * channel_idx % frame_len).astype(jnp.float32) * (2.0 * math.pi / frame_len)
    table = jnp.stack([jnp.cos(phase), -jnp.sin(phase)], axis=2)
    return table.reshape(frame_len, frame_len).astype(jnp.bfloat16)


def per_device(voltages):
    inputs_here = voltages.shape[0]
    frame_len = 2 * CH
    frames = voltages.reshape(inputs_here, voltages.shape[1] // frame_len, frame_len)
    spectra_here = frames.shape[1]
    last_frames = frames[:, spectra_here - (TAPS - 1) :, :]
    history = shifted(last_frames, ("tm", "pol"), 1)
    extended = jnp.concatenate([history, frames], axis=1)
    filter_taps = prototype(TAPS, frame_len)
    filtered = jnp.zeros((inputs_here, spectra_here, frame_len), jnp.float32)
    for tap_index in range(TAPS):
        filtered = filtered + filter_taps[tap_index] * extended[
            :, tap_index : tap_index + spectra_here, :
        ].astype(jnp.float32)
    filtered = filtered.astype(jnp.bfloat16)
    spectra = lax.dot_general(
        dft_table(frame_len),
        filtered.reshape(inputs_here * spectra_here, frame_len),
        (((0,), (1,)), ((), ())),
        preferred_element_type=jnp.float32,
    )
    spectra = spectra.astype(jnp.bfloat16).reshape(CH, 2, inputs_here, spectra_here)
    inp_size = lax.axis_size("inp")
    tm_size = lax.axis_size("tm")
    own_channels = CH // (inp_size * tm_size)
    widened = spectra.reshape(CH, 2, 1, inputs_here, spectra_here)
    received = lax.all_to_all(widened, ("inp", "tm"), split_axis=0, concat_axis=2, tiled=True)
    received = received.reshape(own_channels, 2, inp_size, tm_size, inputs_here, spectra_here)
    turned = received.transpose(0, 1, 2, 4, 3, 5).reshape(
        own_channels, 2, inp_size * inputs_here, tm_size * spectra_here
    )
    pol_size = lax.axis_size("pol")
    rows_here = turned.shape[2] // pol_size
    row_start = lax.axis_index("pol") * rows_here
    segment = lax.all_gather(turned, "pol", axis=3, tiled=True)
    own_rows = lax.dynamic_slice_in_dim(segment, row_start, rows_here, 2)
    left_rows = jnp.concatenate([own_rows[:, 0], own_rows[:, 1]], axis=-1)
    right_real = jnp.concatenate([segment[:, 0], segment[:, 1]], axis=-1)
    right_imag = jnp.concatenate([-segment[:, 1], segment[:, 0]], axis=-1)
    part_real = jnp.einsum(
        "crk,cjk->crj", left_rows, right_real, preferred_element_type=jnp.float32
    )
    part_imag = jnp.einsum(
        "crk,cjk->crj", left_rows, right_imag, preferred_element_type=jnp.float32
    )
    summed = jnp.stack([part_real, part_imag], axis=1)
    return summed * (1.0 / (turned.shape[3] * pol_size))


def solution(mesh):
    return jax.shard_map(
        per_device,
        mesh=mesh,
        in_specs=(P(("group", "inp"), ("tm", "pol")),),
        out_specs=P(("group", "inp", "tm"), None, "pol", None),
        check_vma=False,
    )
```

profile of v0, /device:TPU:0, one launch (start us, length us, event | category | flops | bytes accessed | tf_op | source)
XLA Modules:
  0.0 484.7 jit_solution(11061835007359937390)
XLA Ops:
  6.5 0.0 all-gather.2.cloned.1.call-start
  6.5 6.4 %copy.27 = bf16[128,16384]{0,1:T(8,128)(2,1)} copy(bf16[128,16384]{1,0:T(8,128)(2,1)} %param.1) | data formatting | bytes 8388608 | tf_op args[0]
  12.9 4.3 slice.163
  17.2 6.3 %copy.28 = bf16[128,15,1024]{2,0,1:T(8,128)(2,1)} copy(bf16[128,15,1024]{0,2,1:T(8,128)(2,1)} %slice.163) | data formatting | bytes 7864320 | tf_op jit(solution)/shard_map/slice | solution.py:41
  23.5 4.2 collective-permute-start
  27.8 1.1 multiply_reduce_fusion
  29.5 8.5 %negate_convert_fusion = (bf16[1024,512,1]{1,0,2:T(8,128)(2,1)S(1)}, bf16[1024,512,1]{1,0,2:T(8,128)(2,1)S(1)}) fusion(), kind=kLoop, calls=%fused_computation.62 | loop fusion | flops 8912896 | bytes 2097152 | tf_op jit(solution)/shard_map/convert.1
  38.1 0.2 pad_maximum_fusion.2
  38.3 4.1 copy.26
  42.4 2.7 convert_element_type.86
  45.1 0.5 broadcast_divide_fusion
  45.6 0.0 collective-permute-done
  45.6 6.2 %copy.29 = bf16[128,15,1024]{0,2,1:T(8,128)(2,1)} copy(bf16[128,15,1024]{2,0,1:T(8,128)(2,1)} %collective-permute-done) | data formatting | bytes 7864320 | tf_op jit(solution)/shard_map/ppermute | solution.py:14
  51.8 24.9 %add_convert_fusion = bf16[128,16,1024]{0,2,1:T(8,128)(2,1)} fusion(bf16[128,16,1024]{0,2,1:T(8,128)(2,1)} %bitcast.32, bf16[128,15,1024]{0,2,1:T(8,128)(2,1)} %copy.29, f32[1024]{0:T(1024)S(1)} %get-tuple-element.10, f32[1024]{0:T(1024)S(1)} %get-tuple-element.11, f32[1024]{0:T(1024)S(1)} %get-tuple-element.12, f32[1024]{0:T(1024)S(1)} %get-tuple-element.13, ...), kind=kLoop, calls=%fused_computation.37 | loop fusion | flops 132120576 | bytes 12386304 | tf_op jit(solution)/shard_map/convert_element_type | solution.py:50
  76.7 6.7 %copy.30 = bf16[128,16,1024]{2,1,0:T(8,128)(2,1)} copy(bf16[128,16,1024]{0,2,1:T(8,128)(2,1)} %add_convert_fusion) | data formatting | bytes 8388608 | tf_op jit(solution)/shard_map/convert_element_type | solution.py:50
  83.4 8.3 %convolution_convert_fusion = bf16[1024,2048]{1,0:T(8,128)(2,1)} fusion(bf16[1024,1024]{0,1:T(8,128)(2,1)S(1)} %convert_element_type.86, bf16[2048,1024]{1,0:T(8,128)(2,1)} %bitcast.34), kind=kOutput, calls=%fused_computation.54 | convolution fusion | flops 4297064448 | bytes 10485760 | tf_op jit(solution)/shard_map/dot_general | solution.py:51
  91.7 31.6 %reshape_reshape.3 = bf16[512,2,1,128,16]{4,3,1,0,2:T(8,128)(2,1)} reshape(bf16[1024,2048]{1,0:T(8,128)(2,1)} %convolution_convert_fusion) | data formatting | bytes 8388608 | tf_op jit(solution)/shard_map/reshape;reshape | solution.py:61
  123.2 24.9 %copy.31 = bf16[512,2,1,128,16]{3,4,2,1,0:T(8,128)(2,1)} copy(bf16[512,2,1,128,16]{4,3,1,0,2:T(8,128)(2,1)} %reshape_reshape.3) | data formatting | bytes 8388608 | tf_op jit(solution)/shard_map/reshape;reshape | solution.py:61
  148.1 124.0 %all_to_all.15 = bf16[512,2,1,128,16]{3,4,2,1,0:T(8,128)(2,1)S(1)} all-to-all(bf16[512,2,1,128,16]{3,4,2,1,0:T(8,128)(2,1)} %copy.31), channel_id=1, replica_groups=mesh['group'=2,'inp'=4,'tm'=2,'pol'=2] {'inp','tm'}, dimensions={0} | all-to-all | bytes 8388608 | tf_op jit(solution)/shard_map/all_to_all | solution.py:62
  272.1 5.3 %copy.40 = bf16[64,2,4,128,2,16]{3,2,0,1,5,4:T(4,128)(2,1)} copy(bf16[64,2,4,128,2,16]{3,5,1,0,4,2:T(8,128)(2,1)S(1)} %bitcast.33) | data formatting | bytes 8388608 | tf_op jit(solution)/shard_map/reshape | solution.py:64
  277.4 7.2 %reshape.135 = bf16[64,2,512,32]{2,0,1,3:T(8,128)(2,1)} reshape(bf16[64,2,4,128,2,16]{3,2,0,1,5,4:T(4,128)(2,1)} %copy.40) | data formatting | bytes 8388608 | tf_op jit(solution)/shard_map/reshape | solution.py:64
  284.6 0.0 all-gather.2.cloned.1.call-update
  284.6 19.0 %all-gather.2.cloned.1.call-done = bf16[64,2,512,64]{2,0,1,3:T(8,128)(2,1)} async-done(((bf16[64,2,512,32]{2,0,1,3:T(8,128)(2,1)}), bf16[64,2,512,64]{2,0,1,3:T(8,128)(2,1)}) %all-gather.2.cloned.1.call-update) | async-done | bytes 8388624 | tf_op jit(solution)/shard_map/all_gather | solution.py:70
  303.7 4.0 constant_dynamic-slice_fusion
  307.7 5.3 %copy.43 = bf16[64,1,256,64]{3,2,0,1:T(8,128)(2,1)} copy(bf16[64,1,256,64]{2,0,1,3:T(8,128)(2,1)} %get-tuple-element.5) | data formatting | bytes 4194304
  313.1 6.1 %fusion.29 = (bf16[64,1,512,64]{2,0,1,3:T(8,128)(2,1)}, bf16[64,1,512,64]{2,0,1,3:T(8,128)(2,1)}) fusion(bf16[64,2,512,64]{2,0,1,3:T(8,128)(2,1)} %all-gather.2.cloned.1.call-done), kind=kLoop, calls=%fused_computation.76 | loop fusion | bytes 16777216 | tf_op jit(solution)/shard_map/slice | solution.py:73
  319.2 9.2 %copy.46 = bf16[64,1,512,64]{3,2,0,1:T(8,128)(2,1)} copy(bf16[64,1,512,64]{2,0,1,3:T(8,128)(2,1)} %get-tuple-element.7) | data formatting | bytes 8388608
  328.4 3.8 copy.44
  332.2 7.7 %bitcast_negate_fusion = bf16[64,512,64]{2,1,0:T(8,128)(2,1)} fusion(bf16[64,1,512,64]{3,2,0,1:T(8,128)(2,1)} %copy.46), kind=kLoop, calls=%fused_computation.75 | loop fusion | flops 2097152 | bytes 8388608 | tf_op jit(solution)/shard_map/neg | solution.py:74
  339.9 9.3 %copy.45 = bf16[64,1,512,64]{3,2,0,1:T(8,128)(2,1)} copy(bf16[64,1,512,64]{2,0,1,3:T(8,128)(2,1)} %get-tuple-element.8) | data formatting | bytes 8388608
  349.2 0.0 copy-start
  349.2 22.8 %convolution_bitcast_fusion = f32[64,1,256,512]{3,2,0,1:T(8,128)} fusion(bf16[64,512,64]{2,1,0:T(8,128)(2,1)} %bitcast.24, bf16[64,512,64]{2,1,0:T(8,128)(2,1)} %bitcast_negate_fusion, bf16[64,256,64]{2,1,0:T(8,128)(2,1)} %bitcast.29, bf16[64,256,64]{2,1,0:T(8,128)(2,1)} %bitcast.27), kind=kOutput, calls=%fused_computation.29 | convolution fusion | flops 2172649472 | bytes 46137344 | tf_op jit(solution)/shard_map/crk,cjk->crj/dot_general | solution.py:78
  371.9 0.0 copy-done
  371.9 18.3 %convolution_bitcast_fusion.1 = f32[64,1,256,512]{3,2,0,1:T(8,128)} fusion(bf16[64,512,64]{2,1,0:T(8,128)(2,1)} %bitcast.26, bf16[64,512,64]{2,1,0:T(8,128)(2,1)S(1)} %bitcast.25, bf16[64,256,64]{2,1,0:T(8,128)(2,1)} %bitcast.30, bf16[64,256,64]{2,1,0:T(8,128)(2,1)} %bitcast.28), kind=kOutput, calls=%fused_computation.30 | convolution fusion | flops 2172649472 | bytes 46137344 | tf_op jit(solution)/shard_map/crk,cjk->crj/dot_general | solution.py:75
  390.3 43.6 %maximum_multiply_fusion = f32[64,2,256,512]{3,2,0,1:T(8,128)} fusion(f32[64,1,256,512]{3,2,0,1:T(8,128)} %convolution_bitcast_fusion, f32[64,1,256,512]{3,2,0,1:T(8,128)} %convolution_bitcast_fusion.1), kind=kLoop, calls=%fused_computation | loop fusion | flops 33554432 | bytes 134217728 | tf_op jit(solution)/shard_map/mul | solution.py:82
  433.9 44.0 %copy.38 = f32[64,2,256,512]{3,2,1,0:T(8,128)} copy(f32[64,2,256,512]{3,2,0,1:T(8,128)} %maximum_multiply_fusion) | data formatting | bytes 134217728 | tf_op jit(solution)/shard_map/mul | solution.py:82
  (1 shorter events, 0.0 us)
Async XLA Ops:
  6.5 297.2 %all-gather.2.cloned.1.call-start = ((), (), s32[]{:S(2)}) async-start(), calls=%async_computation.1 | async-start | bytes 12582912 | tf_op jit(solution)/shard_map/all_gather | solution.py:70
  23.5 22.1 %collective-permute-start = (bf16[128,15,1024]{2,0,1:T(8,128)(2,1)}, bf16[128,15,1024]{2,0,1:T(8,128)(2,1)}, u32[]{:S(2)}, u32[]{:S(2)}) collective-permute-start(bf16[128,15,1024]{2,0,1:T(8,128)(2,1)} %copy.28), channel_id=1, source_target_pairs={{0,1},{1,2},{2,3},{4,5},{5,6},{6,7},{8,9},{9,10},{10,11},{12,13},{... | collective-permute-start | bytes 11796488 | tf_op jit(solution)/shard_map/ppermute | solution.py:14
  349.2 22.8 %copy-start = (bf16[64,1,512,64]{3,2,0,1:T(8,128)(2,1)S(1)}, bf16[64,1,512,64]{3,2,0,1:T(8,128)(2,1)}, u32[]{:S(2)}) copy-start(bf16[64,1,512,64]{3,2,0,1:T(8,128)(2,1)} %copy.45) | copy-start | bytes 12582916
Sparse Core Ops, SparseCore 0:
  284.8 18.8 all-gather.1
where the time goes:
time: 488 us; the launch traced here: 485 us
  local copies, waits for them, and re-layouts  187 us (38%)
  blocking collectives  124 us (25%)
  other arithmetic  86.5 us (18%)
  matrix products  49.4 us (10%)
  waiting for transfers between devices  19.1 us (4%)
  between operations  14.1 us (3%)
    all_to_all x1, blocking collectives, per_device(): lax.all_to_all(widened, ('inp', 'tm'), split_axis=0, concat_axis=2, tiled...  124 us
    another operation x2, local copies, waits for them, and re-layouts, per_device(): widened = spectra.reshape(CH, 2, 1, inputs_here, spectra_here)  56.5 us
    mul x1, local copies, waits for them, and re-layouts, per_device(): return summed * (1.0 / (turned.shape[3] * pol_size))  44 us
    mul x1, other arithmetic, per_device(): return summed * (1.0 / (turned.shape[3] * pol_size))  43.6 us
    unnamed x7, local copies, waits for them, and re-layouts  34 us
    convert_element_type x1, other arithmetic, per_device(): filtered = filtered.astype(jnp.bfloat16)  24.9 us
    dot_general x1, matrix products, per_device(): jnp.einsum('crk,cjk->crj', left_rows, right_imag, preferred_element_type=...  22.8 us
    all_gather x1, waiting for transfers between devices, per_device(): segment = lax.all_gather(turned, 'pol', axis=3, tiled=True)  19 us
  transfers between devices with their start and end apart: 2, of which 1 were waited for; matrix products, arithmetic and copies ran while one was open for 4% of the time, Pallas kernels for 0%

commit v1 on v0

--- a/solution.py
+++ b/solution.py
@@ -6,6 +6,12 @@
 
 CH = 512
 TAPS = 16
+
+
+def advance_the_ways(original, dim_i):
+    a_now = jnp.stack(lax.axis_size("pol") * [original], axis=0)
+    later = lax.all_to_all(a_now, "pol", 0, 0)
+    return jnp.concatenate(later, axis=dim_i)
 
 
 def shifted(block, axis, distance):
@@ -67,7 +73,7 @@
     pol_size = lax.axis_size("pol")
     rows_here = turned.shape[2] // pol_size
     row_start = lax.axis_index("pol") * rows_here
-    segment = lax.all_gather(turned, "pol", axis=3, tiled=True)
+    segment = advance_the_ways(turned, 3)
     own_rows = lax.dynamic_slice_in_dim(segment, row_start, rows_here, 2)
     left_rows = jnp.concatenate([own_rows[:, 0], own_rows[:, 1]], axis=-1)
     right_real = jnp.concatenate([segment[:, 0], segment[:, 1]], axis=-1)

time: 488 us -> 492 us (level)
  blocking collectives: 124 us -> 18.5 us
  waiting for transfers between devices: 19.1 us -> 91.6 us
  starting transfers between devices: 4.24 us -> 36.7 us
  between operations: 14.1 us -> 0.73 us
  local copies, waits for them, and re-layouts: 187 us -> 198 us
  other arithmetic: 86.5 us -> 94.1 us
    all_to_all x1, blocking collectives: 124 us -> 18.5 us  [advance_the_ways(): later = lax.all_to_all(a_now, 'pol', 0, 0)]
    all_to_all x0 -> x1, waiting for transfers between devices: none -> 91.6 us  [per_device(): lax.all_to_all(widened, ('inp', 'tm'), split_axis=0, concat_axis=2, tiled...]
    all_to_all x0 -> x1, starting transfers between devices: none -> 32.5 us  [per_device(): lax.all_to_all(widened, ('inp', 'tm'), split_axis=0, concat_axis=2, tiled...]
    all_gather x1 -> x0, waiting for transfers between devices: 19 us -> none  [per_device(): segment = lax.all_gather(turned, 'pol', axis=3, tiled=True)]
    transpose x0 -> x1, local copies, waits for them, and re-layouts: none -> 9.59 us  [per_device(): received.transpose(0, 1, 2, 4, 3, 5)]
    another operation x1 -> x2, other arithmetic: 8.54 us -> 16.2 us
    another operation x0 -> x1, local copies, waits for them, and re-layouts: none -> 7.18 us  [advance_the_ways(): a_now = jnp.stack(lax.axis_size('pol') * [original], axis=0)]
    reshape x2 -> x1, local copies, waits for them, and re-layouts: 12.5 us -> 8.44 us  [advance_the_ways(): return jnp.concatenate(later, axis=dim_i)]
where the time goes in v1:
time: 492 us; the launch traced here: 489 us
  local copies, waits for them, and re-layouts  198 us (40%)
  other arithmetic  94.1 us (19%)
  waiting for transfers between devices  91.6 us (19%)
  matrix products  49.2 us (10%)
  starting transfers between devices  36.7 us (7%)
  blocking collectives  18.5 us (4%)
    all_to_all x1, waiting for transfers between devices, per_device(): lax.all_to_all(widened, ('inp', 'tm'), split_axis=0, concat_axis=2, tiled...  91.6 us
    another operation x2, local copies, waits for them, and re-layouts, per_device(): widened = spectra.reshape(CH, 2, 1, inputs_here, spectra_here)  56.5 us
    mul x1, local copies, waits for them, and re-layouts, per_device(): return summed * (1.0 / (turned.shape[3] * pol_size))  44 us
    mul x1, other arithmetic, per_device(): return summed * (1.0 / (turned.shape[3] * pol_size))  43.6 us
    unnamed x9, local copies, waits for them, and re-layouts  33 us
    all_to_all x1, starting transfers between devices, per_device(): lax.all_to_all(widened, ('inp', 'tm'), split_axis=0, concat_axis=2, tiled...  32.5 us
    convert_element_type x1, other arithmetic, per_device(): filtered = filtered.astype(jnp.bfloat16)  24.9 us
    dot_general x1, matrix products, per_device(): jnp.einsum('crk,cjk->crj', left_rows, right_imag, preferred_element_type=...  22.8 us
  transfers between devices with their start and end apart: 2, of which 1 were waited for; matrix products, arithmetic and copies ran while one was open for 4% of the time, Pallas kernels for 0%

profile of v1, /device:TPU:0, one launch (start us, length us, event | category | flops | bytes accessed | tf_op | source)
XLA Modules:
  0.0 488.6 jit_solution(15606624826247650392)
XLA Ops:
  0.0 6.4 %copy.36 = bf16[128,16384]{0,1:T(8,128)(2,1)} copy(bf16[128,16384]{1,0:T(8,128)(2,1)} %param.1) | data formatting | bytes 8388608 | tf_op args[0]
  6.4 4.3 slice.163
  10.7 6.3 %copy.37 = bf16[128,15,1024]{2,0,1:T(8,128)(2,1)} copy(bf16[128,15,1024]{0,2,1:T(8,128)(2,1)} %slice.163) | data formatting | bytes 7864320 | tf_op jit(solution)/shard_map/slice | solution.py:47
  17.0 4.2 collective-permute-start
  21.2 1.1 multiply_reduce_fusion
  23.0 8.5 %negate_convert_fusion = (bf16[1024,512,1]{1,0,2:T(8,128)(2,1)S(1)}, bf16[1024,512,1]{1,0,2:T(8,128)(2,1)S(1)}) fusion(), kind=kLoop, calls=%fused_computation.63 | loop fusion | flops 8912896 | bytes 2097152 | tf_op jit(solution)/shard_map/convert.1
  31.6 0.2 pad_maximum_fusion.3
  31.8 4.1 copy.35
  35.8 2.7 convert_element_type.86
  38.6 0.5 broadcast_divide_fusion
  39.1 0.0 collective-permute-done
  39.1 6.2 %copy.38 = bf16[128,15,1024]{0,2,1:T(8,128)(2,1)} copy(bf16[128,15,1024]{2,0,1:T(8,128)(2,1)} %collective-permute-done) | data formatting | bytes 7864320 | tf_op jit(solution)/shard_map/ppermute | solution.py:20
  45.2 24.9 %add_convert_fusion = bf16[128,16,1024]{0,2,1:T(8,128)(2,1)} fusion(bf16[128,16,1024]{0,2,1:T(8,128)(2,1)} %bitcast.36, bf16[128,15,1024]{0,2,1:T(8,128)(2,1)} %copy.38, f32[1024]{0:T(1024)S(1)} %get-tuple-element.10, f32[1024]{0:T(1024)S(1)} %get-tuple-element.11, f32[1024]{0:T(1024)S(1)} %get-tuple-element.12, f32[1024]{0:T(1024)S(1)} %get-tuple-element.13, ...), kind=kLoop, calls=%fused_computation.38 | loop fusion | flops 132120576 | bytes 12386304 | tf_op jit(solution)/shard_map/convert_element_type | solution.py:56
  70.2 6.7 %copy.39 = bf16[128,16,1024]{2,1,0:T(8,128)(2,1)} copy(bf16[128,16,1024]{0,2,1:T(8,128)(2,1)} %add_convert_fusion) | data formatting | bytes 8388608 | tf_op jit(solution)/shard_map/convert_element_type | solution.py:56
  76.9 8.3 %convolution_convert_fusion = bf16[1024,2048]{1,0:T(8,128)(2,1)} fusion(bf16[1024,1024]{0,1:T(8,128)(2,1)S(1)} %convert_element_type.86, bf16[2048,1024]{1,0:T(8,128)(2,1)} %bitcast.38), kind=kOutput, calls=%fused_computation.55 | convolution fusion | flops 4297064448 | bytes 10485760 | tf_op jit(solution)/shard_map/dot_general | solution.py:57
  85.1 31.6 %reshape_reshape.3 = bf16[512,2,1,128,16]{4,3,1,0,2:T(8,128)(2,1)} reshape(bf16[1024,2048]{1,0:T(8,128)(2,1)} %convolution_convert_fusion) | data formatting | bytes 8388608 | tf_op jit(solution)/shard_map/reshape;reshape | solution.py:67
  116.7 24.9 %copy.40 = bf16[512,2,1,128,16]{3,4,2,1,0:T(8,128)(2,1)} copy(bf16[512,2,1,128,16]{4,3,1,0,2:T(8,128)(2,1)} %reshape_reshape.3) | data formatting | bytes 8388608 | tf_op jit(solution)/shard_map/reshape;reshape | solution.py:67
  141.6 32.5 %all-to-all-start = ((bf16[512,2,1,128,16]{3,4,2,1,0:T(8,128)(2,1)}), bf16[512,2,1,128,16]{3,4,2,1,0:T(8,128)(2,1)}, u32[]{:S(2)}, u32[]{:S(2)}) async-start(bf16[512,2,1,128,16]{3,4,2,1,0:T(8,128)(2,1)} %copy.40), calls=%async_computation | async-start | bytes 8388608 | tf_op jit(solution)/shard_map/all_to_all | solution.py:68
  174.1 91.6 %all-to-all-done = bf16[512,2,1,128,16]{3,4,2,1,0:T(8,128)(2,1)} async-done(((bf16[512,2,1,128,16]{3,4,2,1,0:T(8,128)(2,1)}), bf16[512,2,1,128,16]{3,4,2,1,0:T(8,128)(2,1)}, u32[]{:S(2)}, u32[]{:S(2)}) %all-to-all-start) | async-done | bytes 4194336 | tf_op jit(solution)/shard_map/all_to_all | solution.py:68
  265.7 9.6 %copy.42 = bf16[64,2,4,128,2,16]{3,2,5,4,1,0:T(4,128)(2,1)} copy(bf16[64,2,4,128,2,16]{3,5,1,0,4,2:T(8,128)(2,1)} %bitcast.6) | data formatting | bytes 8388608 | tf_op jit(solution)/shard_map/transpose | solution.py:70
  275.3 7.2 %stack_reshape.4 = bf16[1,64,2,512,32]{3,4,2,1,0:T(8,128)(2,1)} reshape(bf16[64,2,4,128,2,16]{3,2,5,4,1,0:T(4,128)(2,1)} %copy.42) | data formatting | bytes 8388608 | tf_op jit(solution)/shard_map/stack;reshape | solution.py:12
  282.5 7.6 %pad_maximum_fusion = bf16[2,64,2,512,32]{3,4,2,1,0:T(8,128)(2,1)} fusion(bf16[1,64,2,512,32]{3,4,2,1,0:T(8,128)(2,1)} %stack_reshape.4), kind=kLoop, calls=%fused_computation.31 | loop fusion | flops 4194304 | bytes 12582912 | tf_op jit(solution)/shard_map/stack | solution.py:12
  290.1 18.5 %all_to_all.20 = bf16[2,64,2,512,32]{3,4,2,1,0:T(8,128)(2,1)} all-to-all(bf16[2,64,2,512,32]{3,4,2,1,0:T(8,128)(2,1)} %pad_maximum_fusion), channel_id=1, replica_groups=mesh['group'=2,'inp'=4,'tm'=2,'pol'=2] {'pol'}, dimensions={0} | all-to-all | bytes 16777216 | tf_op jit(solution)/shard_map/all_to_all | solution.py:13
  308.6 8.4 %copy.43 = bf16[64,2,512,2,32]{2,4,3,1,0:T(8,128)(2,1)} copy(bf16[64,2,512,2,32]{2,4,1,0,3:T(8,128)(2,1)} %bitcast.37) | data formatting | bytes 16777216 | tf_op jit(solution)/shard_map/reshape | solution.py:14
  317.0 0.0 copy-start.1
  317.0 7.0 %fusion.29 = (bf16[64,1,512,64]{2,3,1,0:T(8,128)(2,1)}, bf16[64,1,512,64]{2,3,1,0:T(8,128)(2,1)}) fusion(bf16[64,2,512,64]{2,3,1,0:T(8,128)(2,1)} %bitcast.29), kind=kLoop, calls=%fused_computation.77 | loop fusion | bytes 16777216 | tf_op jit(solution)/shard_map/slice | solution.py:79
  324.1 1.8 copy-done.1
  325.8 1.7 constant_dynamic-slice_fusion
  327.5 4.9 copy.50
  332.4 8.4 %copy.53 = bf16[64,1,512,64]{3,2,0,1:T(8,128)(2,1)} copy(bf16[64,1,512,64]{2,3,1,0:T(8,128)(2,1)} %get-tuple-element.7) | data formatting | bytes 8388608
  340.8 3.2 copy.51
  344.0 7.7 %bitcast_negate_fusion = bf16[64,512,64]{2,1,0:T(8,128)(2,1)} fusion(bf16[64,1,512,64]{3,2,0,1:T(8,128)(2,1)} %copy.53), kind=kLoop, calls=%fused_computation.76 | loop fusion | flops 2097152 | bytes 8388608 | tf_op jit(solution)/shard_map/neg | solution.py:80
  351.7 8.4 %copy.52 = bf16[64,1,512,64]{3,2,0,1:T(8,128)(2,1)} copy(bf16[64,1,512,64]{2,3,1,0:T(8,128)(2,1)} %get-tuple-element.8) | data formatting | bytes 8388608
  360.1 0.0 copy-start
  360.1 22.8 %convolution_bitcast_fusion = f32[64,1,256,512]{3,2,0,1:T(8,128)} fusion(bf16[64,512,64]{2,1,0:T(8,128)(2,1)} %bitcast.26, bf16[64,512,64]{2,1,0:T(8,128)(2,1)} %bitcast_negate_fusion, bf16[64,256,64]{2,1,0:T(8,128)(2,1)} %bitcast.33, bf16[64,256,64]{2,1,0:T(8,128)(2,1)} %bitcast.31), kind=kOutput, calls=%fused_computation.29 | convolution fusion | flops 2172649472 | bytes 46137344 | tf_op jit(solution)/shard_map/crk,cjk->crj/dot_general | solution.py:84
  382.9 0.0 copy-done
  382.9 18.1 %convolution_bitcast_fusion.1 = f32[64,1,256,512]{3,2,0,1:T(8,128)} fusion(bf16[64,512,64]{2,1,0:T(8,128)(2,1)} %bitcast.28, bf16[64,512,64]{2,1,0:T(8,128)(2,1)S(1)} %bitcast.27, bf16[64,256,64]{2,1,0:T(8,128)(2,1)} %bitcast.34, bf16[64,256,64]{2,1,0:T(8,128)(2,1)} %bitcast.32), kind=kOutput, calls=%fused_computation.30 | convolution fusion | flops 2172649472 | bytes 46137344 | tf_op jit(solution)/shard_map/crk,cjk->crj/dot_general | solution.py:81
  401.0 43.6 %maximum_multiply_fusion = f32[64,2,256,512]{3,2,0,1:T(8,128)} fusion(f32[64,1,256,512]{3,2,0,1:T(8,128)} %convolution_bitcast_fusion, f32[64,1,256,512]{3,2,0,1:T(8,128)} %convolution_bitcast_fusion.1), kind=kLoop, calls=%fused_computation | loop fusion | flops 33554432 | bytes 134217728 | tf_op jit(solution)/shard_map/mul | solution.py:88
  444.6 44.0 %copy.47 = f32[64,2,256,512]{3,2,1,0:T(8,128)} copy(f32[64,2,256,512]{3,2,0,1:T(8,128)} %maximum_multiply_fusion) | data formatting | bytes 134217728 | tf_op jit(solution)/shard_map/mul | solution.py:88
  (1 shorter events, 0.0 us)
Async XLA Ops:
  17.0 22.1 %collective-permute-start = (bf16[128,15,1024]{2,0,1:T(8,128)(2,1)}, bf16[128,15,1024]{2,0,1:T(8,128)(2,1)}, u32[]{:S(2)}, u32[]{:S(2)}) collective-permute-start(bf16[128,15,1024]{2,0,1:T(8,128)(2,1)} %copy.37), channel_id=1, source_target_pairs={{0,1},{1,2},{2,3},{4,5},{5,6},{6,7},{8,9},{9,10},{10,11},{12,13},{... | collective-permute-start | bytes 11796488 | tf_op jit(solution)/shard_map/ppermute | solution.py:20
  141.6 124.1 %all-to-all-start = ((bf16[512,2,1,128,16]{3,4,2,1,0:T(8,128)(2,1)}), bf16[512,2,1,128,16]{3,4,2,1,0:T(8,128)(2,1)}, u32[]{:S(2)}, u32[]{:S(2)}) async-start(bf16[512,2,1,128,16]{3,4,2,1,0:T(8,128)(2,1)} %copy.40), calls=%async_computation | async-start | bytes 8388608 | tf_op jit(solution)/shard_map/all_to_all | solution.py:68
  317.0 8.8 %copy-start.1 = (bf16[64,2,512,2,32]{2,4,3,1,0:T(8,128)(2,1)S(1)}, bf16[64,2,512,2,32]{2,4,3,1,0:T(8,128)(2,1)}, u32[]{:S(2)}) copy-start(bf16[64,2,512,2,32]{2,4,3,1,0:T(8,128)(2,1)} %copy.43) | copy-start | bytes 25165828
  360.1 22.8 %copy-start = (bf16[64,1,512,64]{3,2,0,1:T(8,128)(2,1)S(1)}, bf16[64,1,512,64]{3,2,0,1:T(8,128)(2,1)}, u32[]{:S(2)}) copy-start(bf16[64,1,512,64]{3,2,0,1:T(8,128)(2,1)} %copy.52) | copy-start | bytes 12582916
